TPU v7x, 128 devices: a whole 4x4x4 slice. The times are simulated.
128 devices in a mesh: col: 8 (over y, z_hi), pair: 16 (over x, z_lo, core).
Axes of the slice: x: 4, y: 4, z: 4 (z_hi: 2, z_lo: 2; z = z_hi * 2 + z_lo), core: 2. Of those that a mesh axis runs over, the one named last changes fastest.
Arguments:
- integrals: bfloat16 [512, 128, 128], P('pair', 'col'), may hold values from -6 to 6
- pno_energy: float32 [512, 128], P('pair'), may hold values from 0.5 to 4
- shift: float32 [512], P('pair'), may hold values from 0.5 to 2
- intersections: bfloat16 [512, 128, 128, 128], P('pair', 'col'), may hold values from -0.09375 to 0.09375
- links: int32 [512, 128], P('pair', 'col'), may hold values from 0 to 63
- counts: int32 [512], P('pair'), may hold values from 1 to 128, as said below
- column_of: int32 [512], P('pair'), may hold values from 0 to 63
Outputs:
- amplitudes: float32 [512, 128, 128], P('pair', 'col')
- pair_energy: float32 [512], P('pair')
Inputs may be any that keep to these rules, and one draw needn't show every extreme that they name: Pair p couples through its first counts[p] slots; later slots are unused.
All inputs are finite; a program needn't handle non-finite values.
Results may differ from a plain program's by a relative error of at most 0.0012.
Values may be sent and summed in bfloat16 or wider, within the bound.
No kernel may reach another device: no remote copies, remote signals or barrier semaphores. Data moves between devices by JAX's collectives and lax.ppermute only.
A program may use at most 192 MiB of HBM per device.

v0:
```python
import jax
import jax.numpy as jnp
from jax import lax
from jax.sharding import PartitionSpec as P

COL_DEV = 8
SWEEPS = 3


def per_device(integrals, pno_energy, shift, intersections, links, counts, column_of):
    pair_dev = integrals.shape[0]
    row_count = integrals.shape[1]
    width = integrals.shape[2]
    slot_dev = intersections.shape[1]
    col_size = lax.axis_size("col")
    ncol_all = COL_DEV * col_size
    rank = lax.axis_index("col")
    row_energy = lax.dynamic_slice_in_dim(pno_energy, rank * row_count, row_count, 1)
    denom = row_energy[:, :, None] + pno_energy[:, None, :] + shift[:, None, None]
    kfloat = integrals.astype(jnp.float32)
    amplitudes = -kfloat / denom
    one_hot = (jnp.arange(ncol_all, dtype=jnp.int32)[:, None] == column_of[None, :]).astype(
        jnp.float32
    )
    own_tiles, own_links = (intersections, links)
    slot_ids = rank * slot_dev + jnp.arange(slot_dev, dtype=jnp.int32)
    own_live = (slot_ids[None, :] < counts[:, None]).astype(jnp.float32)
    for sweep in range(SWEEPS):
        contrib = jnp.dot(
            one_hot,
            amplitudes.reshape(pair_dev, row_count * width),
            precision=lax.Precision.HIGHEST,
        )
        contrib = contrib.reshape(ncol_all, row_count, width)
        totals = lax.psum(contrib, "pair")
        colamp = lax.all_gather(totals.astype(jnp.bfloat16), "col", axis=1, tiled=True)
        selected = colamp[own_links]
        left = jnp.einsum(
            "pmab,pmbc->pmac", own_tiles, selected, preferred_element_type=jnp.float32
        ).astype(jnp.bfloat16)
        right = jnp.einsum("pmac,pmdc->pmad", left, own_tiles, preferred_element_type=jnp.float32)
        partial_sum = jnp.sum(right * own_live[:, :, None, None], axis=1)
        coupled = lax.psum_scatter(partial_sum, "col", scatter_dimension=1, tiled=True)
        amplitudes = -(kfloat + coupled) / denom
    pair_energy = lax.psum(jnp.sum(kfloat * amplitudes, axis=(1, 2)), "col")
    return (amplitudes, pair_energy)


def solution(mesh):
    placed = (
        P("pair", "col", None),
        P("pair", None),
        P("pair"),
        P("pair", "col", None, None),
        P("pair", "col"),
        P("pair"),
        P("pair"),
    )
    return jax.shard_map(
        per_device,
        mesh=mesh,
        in_specs=placed,
        out_specs=(P("pair", "col", None), P("pair")),
        check_vma=False,
    )
```

profile of v0, /device:TPU:0, one launch (start us, length us, event | category | flops | bytes accessed | tf_op | source)
XLA Modules:
  0.0 745.7 jit_solution(13268401989379443307)
XLA Ops:
  7.2 0.0 all-gather.4.cloned.1.call-start
  7.2 0.8 constant_dynamic-slice_fusion
  8.0 1.1 fusion.18
  9.1 1.1 fusion.32
  10.3 62.5 %all-reduce.3 = bf16[64,16,128]{2,0,1:T(8,128)(2,1)} all-reduce(f32[64,16,128]{2,0,1:T(8,128)S(1)} %fusion.32), channel_id=1, replica_groups=mesh['col'=8,'pair'=16] {'pair'}, use_global_device_ids=true, to_apply=%region_0.0 | all-reduce | flops 131072 | bytes 786432 | tf_op jit(solution)/shard_map/psum | solution.py:35
  72.7 0.0 all-gather.4.cloned.1.call-update
  72.8 0.0 reduce-scatter.4.cloned.1.call-start
  72.8 0.7 compare_select_fusion
  73.5 0.1 copy.17
  73.6 0.1 reshape.61
  73.7 0.7 compare_convert_fusion
  74.4 52.9 %all-gather.4.cloned.1.call-done = bf16[64,128,128]{2,0,1:T(8,128)(2,1)} async-done(((bf16[64,16,128]{2,0,1:T(8,128)(2,1)}), bf16[64,128,128]{2,0,1:T(8,128)(2,1)}) %all-gather.4.cloned.1.call-update) | async-done | bytes 2097168 | tf_op jit(solution)/shard_map/all_gather | solution.py:36
  127.3 2.9 copy.18
  130.2 13.9 %gather_fusion = bf16[512,128,128]{2,1,0:T(8,128)(2,1)} fusion(bf16[64,128,128]{2,1,0:T(8,128)(2,1)S(1)} %copy.18, s32[1024]{0:T(1024)S(1)} %pad_clamp_fusion), kind=kCustom, calls=%fused_computation | custom fusion | bytes 33556480 | tf_op jit(solution)/shard_map/gather | solution.py:37
  144.1 0.0 copy-start
  144.1 29.2 %multiply_reduce_fusion.2 = f32[32,128,128]{2,1,0:T(8,128)} fusion(f32[32,16]{1,0:T(8,128)S(1)} %compare_convert_fusion, bf16[32,16,128,128]{3,2,1,0:T(8,128)(2,1)} %param.10, bf16[32,16,128,128]{3,2,1,0:T(8,128)(2,1)} %bitcast.57), kind=kOutput, calls=%fused_computation.5 | convolution fusion | flops 4319608832 | bytes 35653632 | tf_op jit(solution)/shard_map/pmac,pmdc->pmad/dot_general | solution.py:41
  173.4 0.0 reduce-scatter.4.cloned.1.call-update
  173.4 0.0 all-gather.6.cloned.1.call-start
  173.4 74.5 %reduce-scatter.4.cloned.1.call-done = f32[32,16,128]{2,1,0:T(8,128)} async-done(((f32[32,128,128]{2,1,0:T(8,128)}), f32[32,16,128]{2,1,0:T(8,128)}) %reduce-scatter.4.cloned.1.call-update) | async-done | bytes 262160 | tf_op jit(solution)/shard_map/reduce_scatter | solution.py:43
  247.9 0.0 copy-done
  247.9 0.0 copy-done.1
  247.9 0.0 copy-done.2
  247.9 1.1 fusion.20
  249.1 0.0 copy-done.3
  249.1 0.5 fusion.29
  249.6 59.6 %all-reduce.4 = bf16[64,16,128]{2,0,1:T(8,128)(2,1)} all-reduce(f32[64,16,128]{2,0,1:T(8,128)S(1)} %fusion.29), channel_id=1, replica_groups=mesh['col'=8,'pair'=16] {'pair'}, use_global_device_ids=true, to_apply=%region_3.0 | all-reduce | flops 131072 | bytes 786432 | tf_op jit(solution)/shard_map/psum | solution.py:35
  309.1 0.0 all-gather.6.cloned.1.call-update
  309.2 0.2 reduce-scatter.6.cloned.1.call-start
  309.4 51.7 %all-gather.6.cloned.1.call-done = bf16[64,128,128]{2,0,1:T(8,128)(2,1)} async-done(((bf16[64,16,128]{2,0,1:T(8,128)(2,1)}), bf16[64,128,128]{2,0,1:T(8,128)(2,1)}) %all-gather.6.cloned.1.call-update) | async-done | bytes 2097168 | tf_op jit(solution)/shard_map/all_gather | solution.py:36
  361.1 2.9 copy.22
  364.0 13.9 %gather_fusion.1 = bf16[512,128,128]{2,1,0:T(8,128)(2,1)} fusion(bf16[64,128,128]{2,1,0:T(8,128)(2,1)S(1)} %copy.22, s32[1024]{0:T(1024)S(1)} %pad_clamp_fusion), kind=kCustom, calls=%fused_computation.1 | custom fusion | bytes 33556480 | tf_op jit(solution)/shard_map/gather | solution.py:37
  377.9 29.2 %multiply_reduce_fusion.1 = f32[32,128,128]{2,1,0:T(8,128)} fusion(f32[32,16]{1,0:T(8,128)S(1)} %compare_convert_fusion, bf16[32,16,128,128]{3,2,1,0:T(8,128)(2,1)} %param.10, bf16[32,16,128,128]{3,2,1,0:T(8,128)(2,1)} %bitcast.58), kind=kOutput, calls=%fused_computation.4 | convolution fusion | flops 4319608832 | bytes 35653632 | tf_op jit(solution)/shard_map/pmac,pmdc->pmad/dot_general | solution.py:41
  407.1 0.0 reduce-scatter.6.cloned.1.call-update
  407.1 0.0 all-gather.8.cloned.1.call-start
  407.2 74.3 %reduce-scatter.6.cloned.1.call-done = f32[32,16,128]{2,1,0:T(8,128)} async-done(((f32[32,128,128]{2,1,0:T(8,128)}), f32[32,16,128]{2,1,0:T(8,128)}) %reduce-scatter.6.cloned.1.call-update) | async-done | bytes 262160 | tf_op jit(solution)/shard_map/reduce_scatter | solution.py:43
  481.5 1.1 fusion.22
  482.7 0.5 fusion.26
  483.2 59.7 %all-reduce.5 = bf16[64,16,128]{2,0,1:T(8,128)(2,1)} all-reduce(f32[64,16,128]{2,0,1:T(8,128)S(1)} %fusion.26), channel_id=1, replica_groups=mesh['col'=8,'pair'=16] {'pair'}, use_global_device_ids=true, to_apply=%region_6.0 | all-reduce | flops 131072 | bytes 786432 | tf_op jit(solution)/shard_map/psum | solution.py:35
  542.8 0.0 all-gather.8.cloned.1.call-update
  542.8 0.3 reduce-scatter.8.cloned.1.call-start
  543.1 51.6 %all-gather.8.cloned.1.call-done = bf16[64,128,128]{2,0,1:T(8,128)(2,1)} async-done(((bf16[64,16,128]{2,0,1:T(8,128)(2,1)}), bf16[64,128,128]{2,0,1:T(8,128)(2,1)}) %all-gather.8.cloned.1.call-update) | async-done | bytes 2097168 | tf_op jit(solution)/shard_map/all_gather | solution.py:36
  594.8 2.9 copy.26
  597.7 13.9 %gather_fusion.2 = bf16[512,128,128]{2,1,0:T(8,128)(2,1)} fusion(bf16[64,128,128]{2,1,0:T(8,128)(2,1)S(1)} %copy.26, s32[1024]{0:T(1024)S(1)} %pad_clamp_fusion), kind=kCustom, calls=%fused_computation.2 | custom fusion | bytes 33556480 | tf_op jit(solution)/shard_map/gather | solution.py:37
  611.6 29.2 %multiply_reduce_fusion = f32[32,128,128]{2,1,0:T(8,128)} fusion(f32[32,16]{1,0:T(8,128)S(1)} %compare_convert_fusion, bf16[32,16,128,128]{3,2,1,0:T(8,128)(2,1)} %param.10, bf16[32,16,128,128]{3,2,1,0:T(8,128)(2,1)} %bitcast.56), kind=kOutput, calls=%fused_computation.3 | convolution fusion | flops 4319608832 | bytes 35653632 | tf_op jit(solution)/shard_map/pmac,pmdc->pmad/dot_general | solution.py:41
  640.8 0.0 reduce-scatter.8.cloned.1.call-update
  640.8 74.3 %reduce-scatter.8.cloned.1.call-done = f32[32,16,128]{2,1,0:T(8,128)} async-done(((f32[32,128,128]{2,1,0:T(8,128)}), f32[32,16,128]{2,1,0:T(8,128)}) %reduce-scatter.8.cloned.1.call-update) | async-done | bytes 262160 | tf_op jit(solution)/shard_map/reduce_scatter | solution.py:43
  715.2 2.2 fusion.25
  717.3 21.5 %psum.31 = f32[32]{0:T(128)} all-reduce(f32[32]{0:T(128)S(1)} %get-tuple-element.2), channel_id=1, replica_groups=mesh['col'=8,'pair'=16] {'col'}, use_global_device_ids=true, to_apply=%region_10.0 | all-reduce | flops 32 | bytes 256 | tf_op jit(solution)/shard_map/psum | solution.py:45
  (5 shorter events, 0.0 us)
Async XLA Ops:
  7.2 120.1 %all-gather.4.cloned.1.call-start = ((), (), s32[]{:S(2)}) async-start(), calls=%async_computation.3 | async-start | bytes 2359296 | tf_op jit(solution)/shard_map/all_gather | solution.py:36
  72.8 175.2 %reduce-scatter.4.cloned.1.call-start = ((), (), s32[]{:S(2)}) async-start(), calls=%async_computation.4 | async-start | bytes 2359296 | tf_op jit(solution)/shard_map/reduce_scatter | solution.py:43
  144.1 103.8 %copy-start = (bf16[32,16,128]{2,1,0:T(8,128)(2,1)S(1)}, bf16[32,16,128]{2,1,0:T(8,128)(2,1)}, u32[]{:S(2)}) copy-start(bf16[32,16,128]{2,1,0:T(8,128)(2,1)} %param.7) | copy-start | bytes 393220
  144.1 103.8 %copy-start.1 = (f32[32,128]{1,0:T(8,128)S(1)}, f32[32,128]{1,0:T(8,128)}, u32[]{:S(2)}) copy-start(f32[32,128]{1,0:T(8,128)} %param.8) | copy-start | bytes 49156
  144.1 103.8 %copy-start.2 = (f32[32]{0:T(128)S(1)}, f32[32]{0:T(128)}, u32[]{:S(2)}) copy-start(f32[32]{0:T(128)} %param.9) | copy-start | bytes 388
  144.1 104.9 %copy-start.3 = (s32[32]{0:T(128)S(1)}, s32[32]{0:T(128)}, u32[]{:S(2)}) copy-start(s32[32]{0:T(128)} %param.13) | copy-start | bytes 388
  173.4 187.7 %all-gather.6.cloned.1.call-start = ((), (), s32[]{:S(2)}) async-start(), calls=%async_computation.5 | async-start | bytes 2359296 | tf_op jit(solution)/shard_map/all_gather | solution.py:36
  309.2 172.4 %reduce-scatter.6.cloned.1.call-start = ((), (), s32[]{:S(2)}) async-start(), calls=%async_computation.6 | async-start | bytes 2359296 | tf_op jit(solution)/shard_map/reduce_scatter | solution.py:43
  407.1 187.6 %all-gather.8.cloned.1.call-start = ((), (), s32[]{:S(2)}) async-start(), calls=%async_computation.7 | async-start | bytes 2359296 | tf_op jit(solution)/shard_map/all_gather | solution.py:36
  542.8 172.3 %reduce-scatter.8.cloned.1.call-start = ((), (), s32[]{:S(2)}) async-start(), calls=%async_computation.8 | async-start | bytes 2359296 | tf_op jit(solution)/shard_map/reduce_scatter | solution.py:43
Sparse Core Ops, SparseCore 0:
  72.9 54.3 all-gather.3
  173.5 74.3 reduce-scatter.3
  309.3 51.7 all-gather.5
  407.3 74.2 reduce-scatter.5
  543.0 51.7 all-gather.7
  640.9 74.1 reduce-scatter.7
where the time goes:
time: 746 us
  waiting for transfers between devices  379 us (51%)
  blocking collectives  203 us (27%)
  matrix products  89.7 us (12%)
  local copies, waits for them, and re-layouts  51.5 us (7%)
  between operations  14.2 us (2%)
    reduce_scatter x3, waiting for transfers between devices, per_device(): lax.psum_scatter(partial_sum, 'col', scatter_dimension=1, tiled=True)  223 us
    psum x3, blocking collectives, per_device(): totals = lax.psum(contrib, 'pair')  182 us
    all_gather x3, waiting for transfers between devices, per_device(): lax.all_gather(totals.astype(jnp.bfloat16), 'col', axis=1, tiled=True)  156 us
    dot_general x3, matrix products, per_device(): jnp.einsum('pmac,pmdc->pmad', left, own_tiles, preferred_element_type=jnp...  87.6 us
    gather x3, local copies, waits for them, and re-layouts, per_device(): selected = colamp[own_links]  41.7 us
    psum x1, blocking collectives, per_device(): pair_energy = lax.psum(jnp.sum(kfloat * amplitudes, axis=(1, 2)), 'col')  21.5 us
  transfers between devices with their start and end apart: 6, of which 6 were waited for; matrix products, arithmetic and copies ran while one was open for 0% of the time, Pallas kernels for 0%

commit v1 on v0

--- a/solution.py
+++ b/solution.py
@@ -2,6 +2,7 @@
 import jax.numpy as jnp
 from jax import lax
 from jax.sharding import PartitionSpec as P
+from jax.lax import all_to_all, axis_size
 
 COL_DEV = 8
 SWEEPS = 3
@@ -33,7 +34,15 @@
         )
         contrib = contrib.reshape(ncol_all, row_count, width)
         totals = lax.psum(contrib, "pair")
-        colamp = lax.all_gather(totals.astype(jnp.bfloat16), "col", axis=1, tiled=True)
+        colamp = jnp.concatenate(
+            all_to_all(
+                jnp.stack(axis_size("col") * [totals.astype(jnp.bfloat16)]),
+                axis_name="col",
+                split_axis=0,
+                concat_axis=0,
+            ),
+            axis=1,
+        )
         selected = colamp[own_links]
         left = jnp.einsum(
             "pmab,pmbc->pmac", own_tiles, selected, preferred_element_type=jnp.float32

time: 746 us -> 675 us (0.905)
  waiting for transfers between devices: 379 us -> 249 us
  blocking collectives: 203 us -> 259 us
    all_gather x3 -> x0, waiting for transfers between devices: 156 us -> none  [per_device(): lax.all_gather(totals.astype(jnp.bfloat16), 'col', axis=1, tiled=True)]
    all_to_all x0 -> x2, blocking collectives: none -> 57.2 us  [per_device(): all_to_all(jnp.stack(axis_size('col') * [totals.astype(jnp.bfloat16)]), a...]
    all_to_all x0 -> x1, waiting for transfers between devices: none -> 23.4 us  [per_device(): all_to_all(jnp.stack(axis_size('col') * [totals.astype(jnp.bfloat16)]), a...]
    all_gather x3 -> x0, local copies, waits for them, and re-layouts: 8.83 us -> none  [per_device(): lax.all_gather(totals.astype(jnp.bfloat16), 'col', axis=1, tiled=True)]
  transfers between devices with their start and end apart: 6 -> 4, of which waited for: 6 -> 4; matrix products, arithmetic and copies ran while one was open for 0% -> 0% of each run, Pallas kernels for 0% -> 0%
where the time goes in v1:
time: 675 us
  blocking collectives  259 us (38%)
  waiting for transfers between devices  249 us (37%)
  matrix products  89.9 us (13%)
  local copies, waits for them, and re-layouts  48.7 us (7%)
  between operations  13.9 us (2%)
  starting transfers between devices  7.5 us (1%)
  other arithmetic  6.93 us (1%)
    reduce_scatter x3, waiting for transfers between devices, per_device(): lax.psum_scatter(partial_sum, 'col', scatter_dimension=1, tiled=True)  225 us
    psum x3, blocking collectives, per_device(): totals = lax.psum(contrib, 'pair')  180 us
    dot_general x3, matrix products, per_device(): jnp.einsum('pmac,pmdc->pmad', left, own_tiles, preferred_element_type=jnp...  87.8 us
    all_to_all x2, blocking collectives, per_device(): all_to_all(jnp.stack(axis_size('col') * [totals.astype(jnp.bfloat16)]), a...  57.2 us
    gather x3, local copies, waits for them, and re-layouts, per_device(): selected = colamp[own_links]  41.7 us
    all_to_all x1, waiting for transfers between devices, per_device(): all_to_all(jnp.stack(axis_size('col') * [totals.astype(jnp.bfloat16)]), a...  23.4 us
    psum x1, blocking collectives, per_device(): pair_energy = lax.psum(jnp.sum(kfloat * amplitudes, axis=(1, 2)), 'col')  21.5 us
  transfers between devices with their start and end apart: 4, of which 4 were waited for; matrix products, arithmetic and copies ran while one was open for 0% of the time, Pallas kernels for 0%

profile of v1, /device:TPU:0, one launch (start us, length us, event | category | flops | bytes accessed | tf_op | source)
XLA Modules:
  0.0 674.9 jit_solution(4426909340379435740)
XLA Ops:
  7.2 0.8 constant_dynamic-slice_fusion
  8.0 1.1 fusion.18
  9.1 1.1 fusion.32
  10.2 62.0 %all-reduce.3 = bf16[64,16,128]{2,0,1:T(8,128)(2,1)S(1)} all-reduce(f32[64,16,128]{2,0,1:T(8,128)S(1)} %fusion.32), channel_id=1, replica_groups=mesh['col'=8,'pair'=16] {'pair'}, use_global_device_ids=true, to_apply=%region_0.0 | all-reduce | flops 131072 | bytes 786432 | tf_op jit(solution)/shard_map/psum | solution.py:36
  72.2 0.2 copy.20
  72.4 1.6 stack.6
  73.9 7.4 %all-to-all-start = ((bf16[8,64,16,128]{3,2,1,0:T(8,128)(2,1)}), bf16[8,64,16,128]{3,2,1,0:T(8,128)(2,1)}, u32[]{:S(2)}, u32[]{:S(2)}) async-start(bf16[8,64,16,128]{3,2,1,0:T(8,128)(2,1)} %stack.6), calls=%async_computation | async-start | bytes 4194304 | tf_op jit(solution)/shard_map/all_to_all | solution.py:38
  81.3 0.0 reduce-scatter.4.cloned.1.call-start
  81.4 0.7 compare_select_fusion
  82.1 0.1 copy.22
  82.1 0.1 reshape.91
  82.2 0.7 compare_convert_fusion
  83.0 23.4 %all-to-all-done = bf16[8,64,16,128]{3,2,1,0:T(8,128)(2,1)} async-done(((bf16[8,64,16,128]{3,2,1,0:T(8,128)(2,1)}), bf16[8,64,16,128]{3,2,1,0:T(8,128)(2,1)}, u32[]{:S(2)}, u32[]{:S(2)}) %all-to-all-start) | async-done | bytes 2097184 | tf_op jit(solution)/shard_map/all_to_all | solution.py:38
  106.4 2.2 copy.21
  108.6 13.9 %gather_fusion = bf16[512,128,128]{2,1,0:T(8,128)(2,1)} fusion(bf16[64,128,128]{2,1,0:T(8,128)(2,1)S(1)} %bitcast.66, s32[1024]{0:T(1024)S(1)} %pad_clamp_fusion), kind=kCustom, calls=%fused_computation | custom fusion | bytes 33556480 | tf_op jit(solution)/shard_map/gather | solution.py:46
  122.5 29.3 %multiply_reduce_fusion.2 = f32[32,128,128]{2,1,0:T(8,128)} fusion(f32[32,16]{1,0:T(8,128)S(1)} %compare_convert_fusion, bf16[32,16,128,128]{3,2,1,0:T(8,128)(2,1)} %param.10, bf16[32,16,128,128]{3,2,1,0:T(8,128)(2,1)} %bitcast.69), kind=kOutput, calls=%fused_computation.5 | convolution fusion | flops 4319608832 | bytes 35653632 | tf_op jit(solution)/shard_map/pmac,pmdc->pmad/dot_general | solution.py:50
  151.8 0.0 reduce-scatter.4.cloned.1.call-update
  151.8 0.0 reduce-scatter.6.cloned.1.call-start
  151.8 77.6 %reduce-scatter.4.cloned.1.call-done = f32[32,16,128]{2,1,0:T(8,128)} async-done(((f32[32,128,128]{2,1,0:T(8,128)}), f32[32,16,128]{2,1,0:T(8,128)}) %reduce-scatter.4.cloned.1.call-update) | async-done | bytes 262160 | tf_op jit(solution)/shard_map/reduce_scatter | solution.py:52
  229.4 0.0 copy-done
  229.4 0.0 copy-done.1
  229.4 0.0 copy-done.2
  229.4 1.1 fusion.20
  230.6 0.0 copy-done.3
  230.6 0.5 fusion.29
  231.1 59.2 %all-reduce.4 = bf16[64,16,128]{2,0,1:T(8,128)(2,1)S(1)} all-reduce(f32[64,16,128]{2,0,1:T(8,128)S(1)} %fusion.29), channel_id=1, replica_groups=mesh['col'=8,'pair'=16] {'pair'}, use_global_device_ids=true, to_apply=%region_3.0 | all-reduce | flops 131072 | bytes 786432 | tf_op jit(solution)/shard_map/psum | solution.py:36
  290.3 0.2 copy.26
  290.5 0.3 stack.7
  290.8 28.6 %all_to_all.15 = bf16[8,64,16,128]{3,2,1,0:T(8,128)(2,1)S(1)} all-to-all(bf16[8,64,16,128]{3,2,1,0:T(8,128)(2,1)S(1)} %stack.7), channel_id=1, replica_groups=mesh['col'=8,'pair'=16] {'col'}, dimensions={0} | all-to-all | bytes 4194304 | tf_op jit(solution)/shard_map/all_to_all | solution.py:38
  319.4 0.6 copy.27
  320.0 13.9 %gather_fusion.1 = bf16[512,128,128]{2,1,0:T(8,128)(2,1)} fusion(bf16[64,128,128]{2,1,0:T(8,128)(2,1)S(1)} %bitcast.67, s32[1024]{0:T(1024)S(1)} %pad_clamp_fusion), kind=kCustom, calls=%fused_computation.1 | custom fusion | bytes 33556480 | tf_op jit(solution)/shard_map/gather | solution.py:46
  333.9 29.3 %multiply_reduce_fusion.1 = f32[32,128,128]{2,1,0:T(8,128)} fusion(f32[32,16]{1,0:T(8,128)S(1)} %compare_convert_fusion, bf16[32,16,128,128]{3,2,1,0:T(8,128)(2,1)} %param.10, bf16[32,16,128,128]{3,2,1,0:T(8,128)(2,1)} %bitcast.70), kind=kOutput, calls=%fused_computation.4 | convolution fusion | flops 4319608832 | bytes 35653632 | tf_op jit(solution)/shard_map/pmac,pmdc->pmad/dot_general | solution.py:50
  363.1 0.0 reduce-scatter.6.cloned.1.call-update
  363.2 0.0 reduce-scatter.8.cloned.1.call-start
  363.2 74.0 %reduce-scatter.6.cloned.1.call-done = f32[32,16,128]{2,1,0:T(8,128)} async-done(((f32[32,128,128]{2,1,0:T(8,128)}), f32[32,16,128]{2,1,0:T(8,128)}) %reduce-scatter.6.cloned.1.call-update) | async-done | bytes 262160 | tf_op jit(solution)/shard_map/reduce_scatter | solution.py:52
  437.2 1.1 fusion.22
  438.3 0.5 fusion.26
  438.8 59.2 %all-reduce.5 = bf16[64,16,128]{2,0,1:T(8,128)(2,1)S(1)} all-reduce(f32[64,16,128]{2,0,1:T(8,128)S(1)} %fusion.26), channel_id=1, replica_groups=mesh['col'=8,'pair'=16] {'pair'}, use_global_device_ids=true, to_apply=%region_6.0 | all-reduce | flops 131072 | bytes 786432 | tf_op jit(solution)/shard_map/psum | solution.py:36
  498.0 0.2 copy.31
  498.2 0.3 stack.8
  498.5 28.6 %all_to_all.16 = bf16[8,64,16,128]{3,2,1,0:T(8,128)(2,1)S(1)} all-to-all(bf16[8,64,16,128]{3,2,1,0:T(8,128)(2,1)S(1)} %stack.8), channel_id=1, replica_groups=mesh['col'=8,'pair'=16] {'col'}, dimensions={0} | all-to-all | bytes 4194304 | tf_op jit(solution)/shard_map/all_to_all | solution.py:38
  527.1 0.6 copy.32
  527.7 13.9 %gather_fusion.2 = bf16[512,128,128]{2,1,0:T(8,128)(2,1)} fusion(bf16[64,128,128]{2,1,0:T(8,128)(2,1)S(1)} %bitcast.65, s32[1024]{0:T(1024)S(1)} %pad_clamp_fusion), kind=kCustom, calls=%fused_computation.2 | custom fusion | bytes 33556480 | tf_op jit(solution)/shard_map/gather | solution.py:46
  541.6 29.3 %multiply_reduce_fusion = f32[32,128,128]{2,1,0:T(8,128)} fusion(f32[32,16]{1,0:T(8,128)S(1)} %compare_convert_fusion, bf16[32,16,128,128]{3,2,1,0:T(8,128)(2,1)} %param.10, bf16[32,16,128,128]{3,2,1,0:T(8,128)(2,1)} %bitcast.68), kind=kOutput, calls=%fused_computation.3 | convolution fusion | flops 4319608832 | bytes 35653632 | tf_op jit(solution)/shard_map/pmac,pmdc->pmad/dot_general | solution.py:50
  570.8 0.0 reduce-scatter.8.cloned.1.call-update
  570.9 73.9 %reduce-scatter.8.cloned.1.call-done = f32[32,16,128]{2,1,0:T(8,128)} async-done(((f32[32,128,128]{2,1,0:T(8,128)}), f32[32,16,128]{2,1,0:T(8,128)}) %reduce-scatter.8.cloned.1.call-update) | async-done | bytes 262160 | tf_op jit(solution)/shard_map/reduce_scatter | solution.py:52
  644.7 2.1 fusion.25
  646.9 21.5 %psum.31 = f32[32]{0:T(128)} all-reduce(f32[32]{0:T(128)S(1)} %get-tuple-element.2), channel_id=1, replica_groups=mesh['col'=8,'pair'=16] {'col'}, use_global_device_ids=true, to_apply=%region_10.0 | all-reduce | flops 32 | bytes 256 | tf_op jit(solution)/shard_map/psum | solution.py:54
  (6 shorter events, 0.0 us)
Async XLA Ops:
  73.9 32.5 %all-to-all-start = ((bf16[8,64,16,128]{3,2,1,0:T(8,128)(2,1)}), bf16[8,64,16,128]{3,2,1,0:T(8,128)(2,1)}, u32[]{:S(2)}, u32[]{:S(2)}) async-start(bf16[8,64,16,128]{3,2,1,0:T(8,128)(2,1)} %stack.6), calls=%async_computation | async-start | bytes 4194304 | tf_op jit(solution)/shard_map/all_to_all | solution.py:38
  81.3 148.1 %reduce-scatter.4.cloned.1.call-start = ((), (), s32[]{:S(2)}) async-start(), calls=%async_computation.6 | async-start | bytes 2359296 | tf_op jit(solution)/shard_map/reduce_scatter | solution.py:52
  122.5 107.0 %copy-start = (bf16[32,16,128]{2,1,0:T(8,128)(2,1)S(1)}, bf16[32,16,128]{2,1,0:T(8,128)(2,1)}, u32[]{:S(2)}) copy-start(bf16[32,16,128]{2,1,0:T(8,128)(2,1)} %param.7) | copy-start | bytes 393220
  122.5 107.0 %copy-start.1 = (f32[32,128]{1,0:T(8,128)S(1)}, f32[32,128]{1,0:T(8,128)}, u32[]{:S(2)}) copy-start(f32[32,128]{1,0:T(8,128)} %param.8) | copy-start | bytes 49156
  122.5 107.0 %copy-start.2 = (f32[32]{0:T(128)S(1)}, f32[32]{0:T(128)}, u32[]{:S(2)}) copy-start(f32[32]{0:T(128)} %param.9) | copy-start | bytes 388
  122.5 108.1 %copy-start.3 = (s32[32]{0:T(128)S(1)}, s32[32]{0:T(128)}, u32[]{:S(2)}) copy-start(s32[32]{0:T(128)} %param.13) | copy-start | bytes 388
  151.8 285.4 %reduce-scatter.6.cloned.1.call-start = ((), (), s32[]{:S(2)}) async-start(), calls=%async_computation.7 | async-start | bytes 2359296 | tf_op jit(solution)/shard_map/reduce_scatter | solution.py:52
  363.2 281.6 %reduce-scatter.8.cloned.1.call-start = ((), (), s32[]{:S(2)}) async-start(), calls=%async_computation.8 | async-start | bytes 2359296 | tf_op jit(solution)/shard_map/reduce_scatter | solution.py:52
Sparse Core Ops, SparseCore 0:
  151.9 77.4 reduce-scatter.3
  363.3 73.8 reduce-scatter.5
  571.0 73.7 reduce-scatter.7
